TPU v7x, 32 devices: a whole 2x2x4 slice. The times are simulated.
32 devices in a mesh: sec: 4 (over y, x), dev: 8 (over z, core).
Axes of the slice: x: 2, y: 2, z: 4, core: 2. Of those that a mesh axis runs over, the one named last changes fastest.
Arguments:
- strain_rows: bfloat16 [65536, 128], P(('sec', 'dev')), may hold values from -6 to 6
- bands: int32 [65536], P(('sec', 'dev')), may hold values from 0 to 15
- damaged: int32 [4096], P(('sec', 'dev')), may hold values from 0 to 2047
- owner: int32 [4096, 1], P(('sec', 'dev')), may hold values from 0 to 31; in each aligned block of 128 rows (0 to 127, 128 to 255, ...) at most 8 rows name the same one
- first_layers: bfloat16 [4096, 4096], P(('sec', 'dev')), may hold values from -0.5 to 0.5
- middle_weight: bfloat16 [4096, 4096], P(None, 'sec'), may hold values from -0.09375 to 0.09375
- out_weight: bfloat16 [4096, 128], P('sec'), may hold values from -0.09375 to 0.09375
- band_scale: float32 [16, 4096], replicated, may hold values from 0.5 to 2
- back_weight: bfloat16 [128, 128], replicated, may hold values from -0.5 to 0.5
Outputs:
- response: bfloat16 [4096, 128], P(('sec', 'dev'))
Inputs may be any that keep to these rules, and one draw needn't show every extreme that they name: Among the 128 rows of one macro device no owner is named more than 8 times, a bound that some block reaches. `damaged`: indices into the listing device's own 2048 points.
All inputs are finite; a program needn't handle non-finite values.
Results may differ from a plain program's by a relative error of at most 0.014.
Values may be sent and summed in bfloat16 or wider, within the bound.
No kernel may reach another device: no remote copies, remote signals or barrier semaphores. Data moves between devices by JAX's collectives and lax.ppermute only.
A program may use at most 128 MiB of HBM per device.

v0:
```python
import jax
import jax.numpy as jnp
from jax import lax
from jax.sharding import PartitionSpec as P

PASSES = 2


def band_rows(band_values, band_scale):
    levels = jnp.arange(band_scale.shape[0], dtype=jnp.float32)
    picks = (band_values.astype(jnp.float32)[:, None] == levels[None, :]).astype(jnp.float32)
    return jnp.dot(
        picks, band_scale, precision=lax.Precision.HIGHEST, preferred_element_type=jnp.float32
    )


def first_hidden(row_block, weight_block, band_block, band_scale):
    mixed = jnp.dot(row_block, weight_block, preferred_element_type=jnp.float32) * band_rows(
        band_block, band_scale
    )
    return jax.nn.silu(mixed).astype(jnp.bfloat16)


def surrogate_tail(hidden_block, middle_weight, out_weight):
    middle = jax.nn.silu(
        jnp.dot(hidden_block, middle_weight, preferred_element_type=jnp.float32)
    ).astype(jnp.bfloat16)
    return jnp.dot(middle, out_weight, preferred_element_type=jnp.float32)


def per_device(
    strain_rows,
    bands,
    damaged,
    owner,
    first_layers,
    middle_weight,
    out_weight,
    band_scale,
    back_weight,
):
    count_all = lax.axis_size(("sec", "dev"))
    list_rows = damaged.shape[0]
    slot_count = max(2, 2 * list_rows // count_all)
    recv_rows = count_all * slot_count
    feat_width = strain_rows.shape[1]
    features = jnp.take(strain_rows, damaged, axis=0)
    band_local = jnp.take(bands, damaged)
    target_owner = owner[:, 0]
    matches = (target_owner[:, None] == jnp.arange(count_all, dtype=jnp.int32)[None, :]).astype(
        jnp.int32
    )
    slot_rank = jnp.sum((jnp.cumsum(matches, axis=0) - 1) * matches, axis=1)
    target = target_owner * slot_count + slot_rank
    dispatch = (jnp.arange(recv_rows, dtype=jnp.int32)[:, None] == target[None, :]).astype(
        jnp.bfloat16
    )
    send_band = jnp.dot(
        dispatch, band_local.astype(jnp.bfloat16)[:, None], preferred_element_type=jnp.float32
    ).astype(jnp.bfloat16)
    result = None
    for segment_index in range(PASSES):
        send_rows = jnp.dot(dispatch, features, preferred_element_type=jnp.float32).astype(
            jnp.bfloat16
        )
        got_rows, got_band = (
            lax.all_to_all(
                send_rows.reshape(count_all, slot_count, feat_width),
                ("sec", "dev"),
                split_axis=0,
                concat_axis=0,
                tiled=True,
            ),
            lax.all_to_all(
                send_band.reshape(count_all, slot_count),
                ("sec", "dev"),
                split_axis=0,
                concat_axis=0,
                tiled=True,
            ),
        )
        got_rows = got_rows.reshape(recv_rows, feat_width)
        got_band = got_band.reshape(recv_rows)
        hidden = first_hidden(got_rows, first_layers, got_band, band_scale)
        every_hidden = lax.all_gather(hidden, "sec", axis=0, tiled=True)
        partial_value = lax.psum_scatter(
            surrogate_tail(every_hidden, middle_weight, out_weight),
            "sec",
            scatter_dimension=0,
            tiled=True,
        )
        response = partial_value.astype(jnp.bfloat16)
        returned = lax.all_to_all(
            response.reshape(count_all, slot_count, response.shape[1]),
            ("sec", "dev"),
            split_axis=0,
            concat_axis=0,
            tiled=True,
        )
        returned = returned.reshape(recv_rows, response.shape[1])
        result = lax.dot_general(
            dispatch, returned, (((0,), (0,)), ((), ())), preferred_element_type=jnp.float32
        ).astype(jnp.bfloat16)
        if segment_index + 1 < PASSES:
            features = (
                features.astype(jnp.float32)
                + jnp.dot(result, back_weight, preferred_element_type=jnp.float32)
            ).astype(jnp.bfloat16)
    return result


def solution(mesh):
    in_specs = (
        P(("sec", "dev"), None),
        P(("sec", "dev")),
        P(("sec", "dev")),
        P(("sec", "dev"), None),
        P(("sec", "dev"), None),
        P(None, "sec"),
        P("sec", None),
        P(),
        P(),
    )
    out_specs = P(("sec", "dev"), None)
    return jax.shard_map(
        per_device, mesh=mesh, in_specs=in_specs, out_specs=out_specs, check_vma=False
    )
```

profile of v0, /device:TPU:0, one launch (start us, length us, event | category | flops | bytes accessed | tf_op | source)
XLA Modules:
  0.0 342.8 jit_solution(10192566044894200866)
XLA Ops:
  6.5 0.0 copy-start
  6.5 0.7 compare_select_fusion
  7.3 0.7 fusion.19
  8.0 0.2 reduce_window_sum.11
  8.2 0.8 select_reduce_fusion
  9.0 0.7 multiply_add_fusion
  9.7 1.6 gather_fusion.1
  11.3 0.8 fusion.5
  12.1 0.7 all_to_all.25
  12.9 7.3 %all-to-all-start.1 = ((bf16[32,1,8]{2,1,0:T(2,128)(2,1)}), bf16[32,1,8]{2,1,0:T(2,128)(2,1)S(1)}, u32[]{:S(2)}, u32[]{:S(2)}) async-start(bf16[32,1,8]{2,1,0:T(2,128)(2,1)} %all_to_all.25), calls=%async_computation.1 | async-start | bytes 32768 | tf_op jit(solution)/shard_map/all_to_all | solution.py:74
  20.2 0.7 compare_and_fusion
  20.9 1.8 gather_fusion
  22.6 0.8 fusion.2
  23.5 3.8 %all-to-all-done.1 = bf16[32,1,8]{2,1,0:T(2,128)(2,1)S(1)} async-done(((bf16[32,1,8]{2,1,0:T(2,128)(2,1)}), bf16[32,1,8]{2,1,0:T(2,128)(2,1)S(1)}, u32[]{:S(2)}, u32[]{:S(2)}) %all-to-all-start.1) | async-done | bytes 544 | tf_op jit(solution)/shard_map/all_to_all | solution.py:74
  27.3 2.6 all-to-all-start
  29.8 0.0 all-gather.3.cloned.1.call-start
  29.9 0.1 convert_reduce_fusion
  30.0 0.1 reshape.65
  30.0 4.7 %fusion.6 = f32[256,4096]{1,0:T(8,128)} fusion(f32[16,4096]{1,0:T(8,128)} %param.16, f32[256]{0:T(256)S(1)} %reshape.65), kind=kOutput, calls=%fused_computation.21 | convolution fusion | flops 201330688 | bytes 4457472 | tf_op jit(solution)/shard_map/dot_general | solution.py:12
  34.8 0.0 copy-start.1
  34.8 2.5 all-to-all-done
  37.2 0.0 copy-done
  37.2 4.9 %multiply_convert_fusion.3 = bf16[256,4096]{1,0:T(8,128)(2,1)} fusion(f32[256,4096]{1,0:T(8,128)} %fusion.6, bf16[128,4096]{1,0:T(8,128)(2,1)S(1)} %copy-done, bf16[32,8,128]{2,1,0:T(8,128)(2,1)S(1)} %all-to-all-done), kind=kOutput, calls=%fused_computation.7 | convolution fusion | flops 274726912 | bytes 7405568 | tf_op jit(solution)/shard_map/dot_general | solution.py:18
  42.2 0.0 all-gather.3.cloned.1.call-update
  42.2 0.0 copy-start.2
  42.2 0.2 reduce-scatter.3.cloned.1.call-start
  42.4 86.2 %all-gather.3.cloned.1.call-done = bf16[1024,4096]{1,0:T(8,128)(2,1)} async-done(((bf16[256,4096]{1,0:T(8,128)(2,1)}), bf16[1024,4096]{1,0:T(8,128)(2,1)}) %all-gather.3.cloned.1.call-update) | async-done | bytes 8388624 | tf_op jit(solution)/shard_map/all_gather | solution.py:85
  128.7 0.0 copy-done.1
  128.7 16.1 %fusion = f32[1024,128]{1,0:T(8,128)} fusion(bf16[1024,128]{1,0:T(8,128)(2,1)S(1)} %copy-done.1, bf16[1024,4096]{1,0:T(8,128)(2,1)} %all-gather.3.cloned.1.call-done, bf16[4096,1024]{1,0:T(8,128)(2,1)} %param.14), kind=kOutput, calls=%fused_computation.8 | convolution fusion | flops 8863612928 | bytes 17563648 | tf_op jit(solution)/shard_map/dot_general | solution.py:28
  144.7 0.0 reduce-scatter.3.cloned.1.call-update
  144.8 0.0 all-gather.5.cloned.1.call-start
  144.8 25.2 %reduce-scatter.3.cloned.1.call-done = f32[256,128]{1,0:T(8,128)} async-done(((f32[1024,128]{1,0:T(8,128)}), f32[256,128]{1,0:T(8,128)}) %reduce-scatter.3.cloned.1.call-update) | async-done | bytes 131088 | tf_op jit(solution)/shard_map/reduce_scatter | solution.py:86
  170.0 0.9 convert_bitcast_fusion.1
  170.9 11.8 %all_to_all.31 = bf16[32,8,128]{2,1,0:T(8,128)(2,1)S(1)} all-to-all(bf16[32,8,128]{2,1,0:T(8,128)(2,1)S(1)} %convert_bitcast_fusion.1), channel_id=1, replica_groups=mesh['sec'=4,'dev'=8] {'sec','dev'}, dimensions={0} | all-to-all | bytes 131072 | tf_op jit(solution)/shard_map/all_to_all | solution.py:93
  182.7 0.0 copy-done.2
  182.7 0.3 fusion.4
  183.0 0.2 fusion.3
  183.2 9.1 %all_to_all.32 = bf16[32,8,128]{2,1,0:T(8,128)(2,1)S(1)} all-to-all(bf16[32,8,128]{2,1,0:T(8,128)(2,1)S(1)} %fusion.3), channel_id=1, replica_groups=mesh['sec'=4,'dev'=8] {'sec','dev'}, dimensions={0} | all-to-all | bytes 131072 | tf_op jit(solution)/shard_map/all_to_all | solution.py:67
  192.3 4.9 %multiply_convert_fusion.1 = bf16[256,4096]{1,0:T(8,128)(2,1)} fusion(f32[256,4096]{1,0:T(8,128)} %fusion.6, bf16[128,4096]{1,0:T(8,128)(2,1)S(1)} %copy-done, bf16[32,8,128]{2,1,0:T(8,128)(2,1)S(1)} %all_to_all.32), kind=kOutput, calls=%fused_computation.5 | convolution fusion | flops 274726912 | bytes 7405568 | tf_op jit(solution)/shard_map/dot_general | solution.py:18
  197.2 0.0 all-gather.5.cloned.1.call-update
  197.2 0.3 reduce-scatter.5.cloned.1.call-start
  197.5 83.9 %all-gather.5.cloned.1.call-done = bf16[1024,4096]{1,0:T(8,128)(2,1)} async-done(((bf16[256,4096]{1,0:T(8,128)(2,1)}), bf16[1024,4096]{1,0:T(8,128)(2,1)}) %all-gather.5.cloned.1.call-update) | async-done | bytes 8388624 | tf_op jit(solution)/shard_map/all_gather | solution.py:85
  281.4 16.1 %fusion.1 = f32[1024,128]{1,0:T(8,128)} fusion(bf16[1024,128]{1,0:T(8,128)(2,1)S(1)} %copy-done.1, bf16[1024,4096]{1,0:T(8,128)(2,1)} %all-gather.5.cloned.1.call-done, bf16[4096,1024]{1,0:T(8,128)(2,1)} %param.14), kind=kOutput, calls=%fused_computation.9 | convolution fusion | flops 8863612928 | bytes 17563648 | tf_op jit(solution)/shard_map/dot_general | solution.py:28
  297.5 0.0 reduce-scatter.5.cloned.1.call-update
  297.5 25.3 %reduce-scatter.5.cloned.1.call-done = f32[256,128]{1,0:T(8,128)} async-done(((f32[1024,128]{1,0:T(8,128)}), f32[256,128]{1,0:T(8,128)}) %reduce-scatter.5.cloned.1.call-update) | async-done | bytes 131088 | tf_op jit(solution)/shard_map/reduce_scatter | solution.py:86
  322.8 0.9 convert_bitcast_fusion
  323.7 11.8 %all_to_all.33 = bf16[32,8,128]{2,1,0:T(8,128)(2,1)S(1)} all-to-all(bf16[32,8,128]{2,1,0:T(8,128)(2,1)S(1)} %convert_bitcast_fusion), channel_id=1, replica_groups=mesh['sec'=4,'dev'=8] {'sec','dev'}, dimensions={0} | all-to-all | bytes 131072 | tf_op jit(solution)/shard_map/all_to_all | solution.py:93
  335.5 0.8 convolution_convert_fusion.2
  (2 shorter events, 0.0 us)
Async XLA Ops:
  6.5 30.7 %copy-start = (bf16[128,4096]{1,0:T(8,128)(2,1)S(1)}, bf16[128,4096]{1,0:T(8,128)(2,1)}, u32[]{:S(2)}) copy-start(bf16[128,4096]{1,0:T(8,128)(2,1)} %param.13) | copy-start | bytes 3145732
  12.9 14.4 %all-to-all-start.1 = ((bf16[32,1,8]{2,1,0:T(2,128)(2,1)}), bf16[32,1,8]{2,1,0:T(2,128)(2,1)S(1)}, u32[]{:S(2)}, u32[]{:S(2)}) async-start(bf16[32,1,8]{2,1,0:T(2,128)(2,1)} %all_to_all.25), calls=%async_computation.1 | async-start | bytes 32768 | tf_op jit(solution)/shard_map/all_to_all | solution.py:74
  27.3 9.9 %all-to-all-start = ((bf16[32,8,128]{2,1,0:T(8,128)(2,1)}), bf16[32,8,128]{2,1,0:T(8,128)(2,1)S(1)}, u32[]{:S(2)}, u32[]{:S(2)}) async-start(bf16[32,8,128]{2,1,0:T(8,128)(2,1)} %fusion.2), calls=%async_computation | async-start | bytes 131072 | tf_op jit(solution)/shard_map/all_to_all | solution.py:67
  29.8 98.8 %all-gather.3.cloned.1.call-start = ((), (), s32[]{:S(2)}) async-start(), calls=%async_computation.7 | async-start | bytes 10485760 | tf_op jit(solution)/shard_map/all_gather | solution.py:85
  34.8 93.9 %copy-start.1 = (bf16[1024,128]{1,0:T(8,128)(2,1)S(1)}, bf16[1024,128]{1,0:T(8,128)(2,1)}, u32[]{:S(2)}) copy-start(bf16[1024,128]{1,0:T(8,128)(2,1)} %param.15) | copy-start | bytes 786436
  42.2 140.5 %copy-start.2 = (bf16[128,128]{1,0:T(8,128)(2,1)S(1)}, bf16[128,128]{1,0:T(8,128)(2,1)}, u32[]{:S(2)}) copy-start(bf16[128,128]{1,0:T(8,128)(2,1)} %param.17) | copy-start | bytes 98308
  42.2 127.8 %reduce-scatter.3.cloned.1.call-start = ((), (), s32[]{:S(2)}) async-start(), calls=%async_computation.8 | async-start | bytes 655360 | tf_op jit(solution)/shard_map/reduce_scatter | solution.py:86
  144.8 136.6 %all-gather.5.cloned.1.call-start = ((), (), s32[]{:S(2)}) async-start(), calls=%async_computation.9 | async-start | bytes 10485760 | tf_op jit(solution)/shard_map/all_gather | solution.py:85
  197.2 125.5 %reduce-scatter.5.cloned.1.call-start = ((), (), s32[]{:S(2)}) async-start(), calls=%async_computation.10 | async-start | bytes 655360 | tf_op jit(solution)/shard_map/reduce_scatter | solution.py:86
Sparse Core Ops, SparseCore 0:
  42.3 86.2 all-gather.2
  144.9 25.0 reduce-scatter.2
  197.4 83.9 all-gather.4
  297.7 25.0 reduce-scatter.4
where the time goes:
time: 343 us
  waiting for transfers between devices  227 us (66%)
  matrix products  49.8 us (15%)
  blocking collectives  32.6 us (10%)
  between operations  13.2 us (4%)
  starting transfers between devices  10.4 us (3%)
  other arithmetic  5.7 us (2%)
  local copies, waits for them, and re-layouts  4.2 us (1%)
    all_gather x2, waiting for transfers between devices, per_device(): every_hidden = lax.all_gather(hidden, 'sec', axis=0, tiled=True)  170 us
    reduce_scatter x2, waiting for transfers between devices, per_device(): lax.psum_scatter(surrogate_tail(every_hidden, middle_weight, out_weight),...  50.5 us
    dot_general x2, matrix products, surrogate_tail(): return jnp.dot(middle, out_weight, preferred_element_type=jnp.float32)  32.2 us
    all_to_all x2, blocking collectives, per_device(): lax.all_to_all(response.reshape(count_all, slot_count, response.shape[1])...  23.6 us
    dot_general x2, matrix products, first_hidden(): jnp.dot(row_block, weight_block, preferred_element_type=jnp.float32)  9.87 us
    all_to_all x1, blocking collectives, per_device(): lax.all_to_all(send_rows.reshape(count_all, slot_count, feat_width), ('se...  9.08 us
    all_to_all x1, starting transfers between devices, per_device(): lax.all_to_all(send_band.reshape(count_all, slot_count), ('sec', 'dev'),...  7.33 us
  transfers between devices with their start and end apart: 6, of which 6 were waited for; matrix products, arithmetic and copies ran while one was open for 2% of the time, Pallas kernels for 0%

commit v1 on v0

--- a/solution.py
+++ b/solution.py
@@ -82,7 +82,25 @@
         got_rows = got_rows.reshape(recv_rows, feat_width)
         got_band = got_band.reshape(recv_rows)
         hidden = first_hidden(got_rows, first_layers, got_band, band_scale)
-        every_hidden = lax.all_gather(hidden, "sec", axis=0, tiled=True)
+        ways, here, step = (lax.axis_size("sec"), lax.axis_index("sec"), hidden.shape[0])
+        shape = [n * ways if d == 0 else n for d, n in enumerate(hidden.shape)]
+        full = lax.dynamic_update_slice_in_dim(
+            jnp.zeros(shape, hidden.dtype), hidden, here * step, axis=0
+        )
+        going_up = going_down = hidden
+        for far in range(1, ways // 2 + 1):
+            going_up = lax.ppermute(going_up, "sec", [(d, (d + 1) % ways) for d in range(ways)])
+            full = lax.dynamic_update_slice_in_dim(
+                full, going_up, (here - far) % ways * step, axis=0
+            )
+            if 2 * far < ways:
+                going_down = lax.ppermute(
+                    going_down, "sec", [(d, (d - 1) % ways) for d in range(ways)]
+                )
+                full = lax.dynamic_update_slice_in_dim(
+                    full, going_down, (here + far) % ways * step, axis=0
+                )
+        every_hidden = full
         partial_value = lax.psum_scatter(
             surrogate_tail(every_hidden, middle_weight, out_weight),
             "sec",

time: 343 us -> 454 us (1.32)
  waiting for transfers between devices: 227 us -> 315 us
  local copies, waits for them, and re-layouts: 4.2 us -> 24.9 us
  starting transfers between devices: 10.4 us -> 15.8 us
    ppermute x0 -> x6, waiting for transfers between devices: none -> 264 us  [the longest x4 178 us: per_device(): lax.ppermute(going_up, 'sec', [(d, (d + 1) % ways) for d in range(ways)])]
    all_gather x2 -> x0, waiting for transfers between devices: 170 us -> none  [per_device(): every_hidden = lax.all_gather(hidden, 'sec', axis=0, tiled=True)]
    dynamic_update_slice x0 -> x6, local copies, waits for them, and re-layouts: none -> 12.1 us  [the longest x4 7.57 us: per_device(): lax.dynamic_update_slice_in_dim(full, going_up, (here - far) % ways * ste...]
    another operation x0 -> x2, local copies, waits for them, and re-layouts: none -> 8.56 us
    ppermute x0 -> x6, starting transfers between devices: none -> 5.86 us  [the longest x2 4.52 us: per_device(): lax.ppermute(going_down, 'sec', [(d, (d - 1) % ways) for d in range(ways)])]
    reduce_scatter x2, waiting for transfers between devices: 50.5 us -> 44.9 us  [per_device(): lax.psum_scatter(surrogate_tail(every_hidden, middle_weight, out_weight),...]
  transfers between devices with their start and end apart: 6 -> 10, of which waited for: 6 -> 10; matrix products, arithmetic and copies ran while one was open for 2% -> 3% of each run, Pallas kernels for 0% -> 0%
where the time goes in v1:
time: 454 us
  waiting for transfers between devices  315 us (69%)
  matrix products  46.1 us (10%)
  blocking collectives  32.6 us (7%)
  local copies, waits for them, and re-layouts  24.9 us (5%)
  starting transfers between devices  15.8 us (3%)
  between operations  13.5 us (3%)
  other arithmetic  5.7 us (1%)
    ppermute x4, waiting for transfers between devices, per_device(): lax.ppermute(going_up, 'sec', [(d, (d + 1) % ways) for d in range(ways)])  178 us
    ppermute x2, waiting for transfers between devices, per_device(): lax.ppermute(going_down, 'sec', [(d, (d - 1) % ways) for d in range(ways)])  85.4 us
    reduce_scatter x2, waiting for transfers between devices, per_device(): lax.psum_scatter(surrogate_tail(every_hidden, middle_weight, out_weight),...  44.9 us
    dot_general x2, matrix products, surrogate_tail(): return jnp.dot(middle, out_weight, preferred_element_type=jnp.float32)  32.2 us
    all_to_all x2, blocking collectives, per_device(): lax.all_to_all(response.reshape(count_all, slot_count, response.shape[1])...  23.6 us
  transfers between devices with their start and end apart: 10, of which 10 were waited for; matrix products, arithmetic and copies ran while one was open for 3% of the time, Pallas kernels for 0%

profile of v1, /device:TPU:0, one launch (start us, length us, event | category | flops | bytes accessed | tf_op | source)
XLA Modules:
  0.0 453.6 jit_solution(16223514607654764197)
XLA Ops:
  6.5 0.0 copy-start
  6.5 0.7 compare_select_fusion
  7.3 0.7 fusion.19
  8.0 0.2 reduce_window_sum.11
  8.2 0.8 select_reduce_fusion
  9.0 0.7 multiply_add_fusion
  9.7 1.6 gather_fusion.1
  11.3 0.8 fusion.5
  12.1 0.7 all_to_all.25
  12.9 7.3 %all-to-all-start.1 = ((bf16[32,1,8]{2,1,0:T(2,128)(2,1)}), bf16[32,1,8]{2,1,0:T(2,128)(2,1)S(1)}, u32[]{:S(2)}, u32[]{:S(2)}) async-start(bf16[32,1,8]{2,1,0:T(2,128)(2,1)} %all_to_all.25), calls=%async_computation.1 | async-start | bytes 32768 | tf_op jit(solution)/shard_map/all_to_all | solution.py:74
  20.2 0.7 compare_and_fusion
  20.9 1.8 gather_fusion
  22.6 0.9 fusion.2
  23.5 3.8 all-to-all-done.1
  27.3 2.6 all-to-all-start
  29.9 0.0 reduce-scatter.3.cloned.1.call-start
  29.9 0.1 convert_reduce_fusion
  30.0 0.1 reshape.65
  30.1 4.7 %fusion.6 = f32[256,4096]{1,0:T(8,128)} fusion(f32[16,4096]{1,0:T(8,128)} %param.16, f32[256]{0:T(256)S(1)} %reshape.65), kind=kOutput, calls=%fused_computation.21 | convolution fusion | flops 201330688 | bytes 4457472 | tf_op jit(solution)/shard_map/dot_general | solution.py:12
  34.8 2.4 all-to-all-done
  37.3 0.0 copy-start.1
  37.3 4.3 broadcast.29.clone
  41.5 0.0 copy-done
  41.5 0.0 copy-done.1
  41.5 3.4 constant_dynamic-update-slice_fusion.6
  45.0 0.7 collective-permute-start
  45.7 2.2 collective-permute-start.1
  47.9 46.7 %collective-permute-done = bf16[256,4096]{1,0:T(8,128)(2,1)S(1)} collective-permute-done((bf16[256,4096]{1,0:T(8,128)(2,1)}, bf16[256,4096]{1,0:T(8,128)(2,1)S(1)}, u32[]{:S(2)}, u32[]{:S(2)}) %collective-permute-start) | collective-permute-done | bytes 2097184 | tf_op jit(solution)/shard_map/ppermute | solution.py:92
  94.6 0.0 collective-permute-start.2
  94.6 1.5 constant_dynamic-update-slice_fusion.5
  96.1 0.0 copy-start.3
  96.1 42.8 %collective-permute-done.1 = bf16[256,4096]{1,0:T(8,128)(2,1)} collective-permute-done((bf16[256,4096]{1,0:T(8,128)(2,1)}, bf16[256,4096]{1,0:T(8,128)(2,1)}, u32[]{:S(2)}, u32[]{:S(2)}) %collective-permute-start.1) | collective-permute-done | bytes 2097184 | tf_op jit(solution)/shard_map/ppermute | solution.py:97
  138.9 3.1 constant_dynamic-update-slice_fusion.4
  142.0 41.7 %collective-permute-done.2 = bf16[256,4096]{1,0:T(8,128)(2,1)} collective-permute-done((bf16[256,4096]{1,0:T(8,128)(2,1)S(1)}, bf16[256,4096]{1,0:T(8,128)(2,1)}, u32[]{:S(2)}, u32[]{:S(2)}) %collective-permute-start.2) | collective-permute-done | bytes 2097184 | tf_op jit(solution)/shard_map/ppermute | solution.py:92
  183.7 3.1 constant_dynamic-update-slice_fusion.3
  186.8 0.0 copy-done.3
  186.8 16.1 %fusion = f32[1024,128]{1,0:T(8,128)} fusion(bf16[1024,128]{1,0:T(8,128)(2,1)S(1)} %copy-done.3, bf16[1024,4096]{1,0:T(8,128)(2,1)} %constant_dynamic-update-slice_fusion.3, bf16[4096,1024]{1,0:T(8,128)(2,1)} %param.14), kind=kOutput, calls=%fused_computation.8 | convolution fusion | flops 8863612928 | bytes 17563648 | tf_op jit(solution)/shard_map/dot_general | solution.py:28
  202.9 0.0 reduce-scatter.3.cloned.1.call-update
  203.0 0.0 reduce-scatter.5.cloned.1.call-start
  203.0 23.1 %reduce-scatter.3.cloned.1.call-done = f32[256,128]{1,0:T(8,128)} async-done(((f32[1024,128]{1,0:T(8,128)}), f32[256,128]{1,0:T(8,128)}) %reduce-scatter.3.cloned.1.call-update) | async-done | bytes 131088 | tf_op jit(solution)/shard_map/reduce_scatter | solution.py:104
  226.1 0.9 convert_bitcast_fusion.1
  227.1 11.8 %all_to_all.31 = bf16[32,8,128]{2,1,0:T(8,128)(2,1)S(1)} all-to-all(bf16[32,8,128]{2,1,0:T(8,128)(2,1)S(1)} %convert_bitcast_fusion.1), channel_id=1, replica_groups=mesh['sec'=4,'dev'=8] {'sec','dev'}, dimensions={0} | all-to-all | bytes 131072 | tf_op jit(solution)/shard_map/all_to_all | solution.py:111
  238.8 0.0 copy-done.4
  238.8 0.3 fusion.4
  239.2 0.2 fusion.3
  239.3 9.1 %all_to_all.32 = bf16[32,8,128]{2,1,0:T(8,128)(2,1)S(1)} all-to-all(bf16[32,8,128]{2,1,0:T(8,128)(2,1)S(1)} %fusion.3), channel_id=1, replica_groups=mesh['sec'=4,'dev'=8] {'sec','dev'}, dimensions={0} | all-to-all | bytes 131072 | tf_op jit(solution)/shard_map/all_to_all | solution.py:67
  248.4 4.3 broadcast.29
  252.7 0.0 copy-done.2
  252.7 2.8 constant_dynamic-update-slice_fusion.2
  255.5 0.6 collective-permute-start.3
  256.1 2.3 collective-permute-start.4
  258.4 46.5 %collective-permute-done.3 = bf16[256,4096]{1,0:T(8,128)(2,1)S(1)} collective-permute-done((bf16[256,4096]{1,0:T(8,128)(2,1)S(1)}, bf16[256,4096]{1,0:T(8,128)(2,1)S(1)}, u32[]{:S(2)}, u32[]{:S(2)}) %collective-permute-start.3) | collective-permute-done | bytes 2097184 | tf_op jit(solution)/shard_map/ppermute | solution.py:92
  304.9 0.0 collective-permute-start.5
  304.9 1.5 constant_dynamic-update-slice_fusion.1
  306.4 42.7 %collective-permute-done.4 = bf16[256,4096]{1,0:T(8,128)(2,1)S(1)} collective-permute-done((bf16[256,4096]{1,0:T(8,128)(2,1)S(1)}, bf16[256,4096]{1,0:T(8,128)(2,1)S(1)}, u32[]{:S(2)}, u32[]{:S(2)}) %collective-permute-start.4) | collective-permute-done | bytes 2097184 | tf_op jit(solution)/shard_map/ppermute | solution.py:97
  349.0 1.4 constant_dynamic-update-slice_fusion
  350.5 43.4 %collective-permute-done.5 = bf16[256,4096]{1,0:T(8,128)(2,1)S(1)} collective-permute-done((bf16[256,4096]{1,0:T(8,128)(2,1)S(1)}, bf16[256,4096]{1,0:T(8,128)(2,1)S(1)}, u32[]{:S(2)}, u32[]{:S(2)}) %collective-permute-start.5) | collective-permute-done | bytes 2097184 | tf_op jit(solution)/shard_map/ppermute | solution.py:92
  393.9 1.5 constant_dynamic-update-slice_fusion.7
  395.4 16.1 %fusion.1 = f32[1024,128]{1,0:T(8,128)} fusion(bf16[1024,128]{1,0:T(8,128)(2,1)S(1)} %copy-done.3, bf16[1024,4096]{1,0:T(8,128)(2,1)} %constant_dynamic-update-slice_fusion.7, bf16[4096,1024]{1,0:T(8,128)(2,1)} %param.14), kind=kOutput, calls=%fused_computation.9 | convolution fusion | flops 8863612928 | bytes 17563648 | tf_op jit(solution)/shard_map/dot_general | solution.py:28
  411.5 0.0 reduce-scatter.5.cloned.1.call-update
  411.5 21.7 %reduce-scatter.5.cloned.1.call-done = f32[256,128]{1,0:T(8,128)} async-done(((f32[1024,128]{1,0:T(8,128)}), f32[256,128]{1,0:T(8,128)}) %reduce-scatter.5.cloned.1.call-update) | async-done | bytes 131088 | tf_op jit(solution)/shard_map/reduce_scatter | solution.py:104
  433.2 0.9 convert_bitcast_fusion
  434.1 11.8 %all_to_all.33 = bf16[32,8,128]{2,1,0:T(8,128)(2,1)S(1)} all-to-all(bf16[32,8,128]{2,1,0:T(8,128)(2,1)S(1)} %convert_bitcast_fusion), channel_id=1, replica_groups=mesh['sec'=4,'dev'=8] {'sec','dev'}, dimensions={0} | all-to-all | bytes 131072 | tf_op jit(solution)/shard_map/all_to_all | solution.py:111
  445.9 0.8 convolution_convert_fusion.2
  (4 shorter events, 0.0 us)
Async XLA Ops:
  6.5 35.0 %copy-start = (bf16[128,4096]{1,0:T(8,128)(2,1)S(1)}, bf16[128,4096]{1,0:T(8,128)(2,1)}, u32[]{:S(2)}) copy-start(bf16[128,4096]{1,0:T(8,128)(2,1)} %param.13) | copy-start | bytes 3145732
  12.9 14.4 %all-to-all-start.1 = ((bf16[32,1,8]{2,1,0:T(2,128)(2,1)}), bf16[32,1,8]{2,1,0:T(2,128)(2,1)S(1)}, u32[]{:S(2)}, u32[]{:S(2)}) async-start(bf16[32,1,8]{2,1,0:T(2,128)(2,1)} %all_to_all.25), calls=%async_computation.1 | async-start | bytes 32768 | tf_op jit(solution)/shard_map/all_to_all | solution.py:74
  27.3 10.0 %all-to-all-start = ((bf16[32,8,128]{2,1,0:T(8,128)(2,1)}), bf16[32,8,128]{2,1,0:T(8,128)(2,1)S(1)}, u32[]{:S(2)}, u32[]{:S(2)}) async-start(bf16[32,8,128]{2,1,0:T(8,128)(2,1)} %fusion.2), calls=%async_computation | async-start | bytes 131072 | tf_op jit(solution)/shard_map/all_to_all | solution.py:67
  29.9 196.3 %reduce-scatter.3.cloned.1.call-start = ((), (), s32[]{:S(2)}) async-start(), calls=%async_computation.7 | async-start | bytes 655360 | tf_op jit(solution)/shard_map/reduce_scatter | solution.py:104
  37.3 4.3 copy-start.1
  45.0 49.6 %collective-permute-start = (bf16[256,4096]{1,0:T(8,128)(2,1)}, bf16[256,4096]{1,0:T(8,128)(2,1)S(1)}, u32[]{:S(2)}, u32[]{:S(2)}) collective-permute-start(bf16[256,4096]{1,0:T(8,128)(2,1)} %get-tuple-element.6), channel_id=1, source_target_pairs={{0,8},{8,16},{16,24},{24,0},{1,9},{9,17},{17,25},{25,1},{2,10},{10... | collective-permute-start | bytes 6291464 | tf_op jit(solution)/shard_map/ppermute | solution.py:92
  45.7 93.2 %collective-permute-start.1 = (bf16[256,4096]{1,0:T(8,128)(2,1)}, bf16[256,4096]{1,0:T(8,128)(2,1)}, u32[]{:S(2)}, u32[]{:S(2)}) collective-permute-start(bf16[256,4096]{1,0:T(8,128)(2,1)} %get-tuple-element.6), channel_id=1, source_target_pairs={{0,24},{8,0},{16,8},{24,16},{1,25},{9,1},{17,9},{25,17},{2,26},{10... | collective-permute-start | bytes 6291464 | tf_op jit(solution)/shard_map/ppermute | solution.py:97
  94.6 89.1 %collective-permute-start.2 = (bf16[256,4096]{1,0:T(8,128)(2,1)S(1)}, bf16[256,4096]{1,0:T(8,128)(2,1)}, u32[]{:S(2)}, u32[]{:S(2)}) collective-permute-start(bf16[256,4096]{1,0:T(8,128)(2,1)S(1)} %collective-permute-done), channel_id=1, source_target_pairs={{0,8},{8,16},{16,24},{24,0},{1,9},{9,17},{17,25},{25,1},{2,10},{10... | collective-permute-start | bytes 6291464 | tf_op jit(solution)/shard_map/ppermute | solution.py:92
  96.1 90.8 %copy-start.3 = (bf16[1024,128]{1,0:T(8,128)(2,1)S(1)}, bf16[1024,128]{1,0:T(8,128)(2,1)}, u32[]{:S(2)}) copy-start(bf16[1024,128]{1,0:T(8,128)(2,1)} %param.15) | copy-start | bytes 786436
  186.8 52.0 %copy-start.4 = (bf16[128,128]{1,0:T(8,128)(2,1)S(1)}, bf16[128,128]{1,0:T(8,128)(2,1)}, u32[]{:S(2)}) copy-start(bf16[128,128]{1,0:T(8,128)(2,1)} %param.17) | copy-start | bytes 98308
  203.0 230.3 %reduce-scatter.5.cloned.1.call-start = ((), (), s32[]{:S(2)}) async-start(), calls=%async_computation.8 | async-start | bytes 655360 | tf_op jit(solution)/shard_map/reduce_scatter | solution.py:104
  248.4 4.3 copy-start.2
  255.5 49.4 %collective-permute-start.3 = (bf16[256,4096]{1,0:T(8,128)(2,1)S(1)}, bf16[256,4096]{1,0:T(8,128)(2,1)S(1)}, u32[]{:S(2)}, u32[]{:S(2)}) collective-permute-start(bf16[256,4096]{1,0:T(8,128)(2,1)S(1)} %get-tuple-element.8), channel_id=1, source_target_pairs={{0,8},{8,16},{16,24},{24,0},{1,9},{9,17},{17,25},{25,1},{2,10},{10... | collective-permute-start | bytes 6291464 | tf_op jit(solution)/shard_map/ppermute | solution.py:92
  256.1 92.9 %collective-permute-start.4 = (bf16[256,4096]{1,0:T(8,128)(2,1)S(1)}, bf16[256,4096]{1,0:T(8,128)(2,1)S(1)}, u32[]{:S(2)}, u32[]{:S(2)}) collective-permute-start(bf16[256,4096]{1,0:T(8,128)(2,1)S(1)} %get-tuple-element.8), channel_id=1, source_target_pairs={{0,24},{8,0},{16,8},{24,16},{1,25},{9,1},{17,9},{25,17},{2,26},{10... | collective-permute-start | bytes 6291464 | tf_op jit(solution)/shard_map/ppermute | solution.py:97
  304.9 89.0 %collective-permute-start.5 = (bf16[256,4096]{1,0:T(8,128)(2,1)S(1)}, bf16[256,4096]{1,0:T(8,128)(2,1)S(1)}, u32[]{:S(2)}, u32[]{:S(2)}) collective-permute-start(bf16[256,4096]{1,0:T(8,128)(2,1)S(1)} %collective-permute-done.3), channel_id=1, source_target_pairs={{0,8},{8,16},{16,24},{24,0},{1,9},{9,17},{17,25},{25,1},{2,10},{10... | collective-permute-start | bytes 6291464 | tf_op jit(solution)/shard_map/ppermute | solution.py:92
Sparse Core Ops, SparseCore 0:
  203.1 23.0 reduce-scatter.2
  411.6 21.5 reduce-scatter.4
